TPU v7x, 128 devices: a whole 4x4x4 slice. The times are simulated.
128 devices in a mesh: seq: 16 (over x_hi, z, core), tp: 8 (over y, x_lo).
Axes of the slice: x: 4 (x_hi: 2, x_lo: 2; x = x_hi * 2 + x_lo), y: 4, z: 4, core: 2. Of those that a mesh axis runs over, the one named last changes fastest.
Arguments:
- tokens: bfloat16 [4, 2048, 4096], P(None, 'seq', 'tp'), may hold values from -6 to 6
- new_tokens: bfloat16 [4, 4096], P(None, 'tp'), may hold values from -6 to 6
- w_qkv: bfloat16 [3, 4096, 4096], P(None, None, 'tp')
- w_out: bfloat16 [4096, 4096], P('tp')
- q_gain: float32 [4096], P('tp'), may hold values from 0.5 to 6
- k_gain: float32 [4096], P('tp'), may hold values from 0.5 to 6
- post_gain: float32 [4096], P('tp'), may hold values from 0.5 to 1.5
- lengths: int32 [4], replicated, may hold values from 1 to 2048, 6144 in all
Outputs:
- hidden_out: bfloat16 [4, 2048, 4096], P(None, 'seq', 'tp')
- new_out: bfloat16 [4, 4096], P(None, 'tp')
Inputs may be any that keep to these rules, and one draw needn't show every extreme that they name: `lengths`: one prompt has exactly 2048 live tokens.
All inputs are finite; a program needn't handle non-finite values.
Results may differ from a plain program's by a relative error of at most 0.012.
The roundings to bfloat16 on the way count: a program that leaves them out, or rounds other values in their place, can miss the bound.
Values may be sent and summed in bfloat16 or wider, within the bound.
No kernel may reach another device: no remote copies, remote signals or barrier semaphores. Data moves between devices by JAX's collectives and lax.ppermute only.
A program may use at most 128 MiB of HBM per device.

v0:
```python
import jax
import jax.numpy as jnp
from jax import lax
from jax.sharding import PartitionSpec as P

HD = 128
rope_base = 500000.0
norm_eps = 1e-06
masked_fill = -1e30


def rotate(values, position):
    half = values.shape[-1] // 2
    freq = rope_base ** (-(jnp.arange(half, dtype=jnp.float32) * 2.0) / values.shape[-1])
    angle = position.astype(jnp.float32)[..., None] * freq
    cosine = jnp.cos(angle)
    sine = jnp.sin(angle)
    lower = values[..., :half]
    upper = values[..., half:]
    return jnp.concatenate([lower * cosine - upper * sine, upper * cosine + lower * sine], -1)


def attend_pair(q_all, k_all, v_all, q_new, k_new, v_new, length):
    count = q_all.shape[0]
    scale = HD ** (-0.5)
    scores = jnp.dot(q_all, k_all.T, preferred_element_type=jnp.float32) * scale
    query_pos = jnp.arange(count, dtype=jnp.int32)[:, None]
    key_pos = jnp.arange(count, dtype=jnp.int32)[None, :]
    valid = (key_pos <= query_pos) & (key_pos < length)
    scores = jnp.where(valid, scores, masked_fill)
    top = jnp.max(scores, -1, keepdims=True)
    weights = jnp.where(valid, jnp.exp(scores - top), 0.0)
    total = jnp.sum(weights, -1, keepdims=True)
    prompt_out = (
        jnp.dot(weights.astype(jnp.bfloat16), v_all, preferred_element_type=jnp.float32) / total
    ).astype(jnp.bfloat16)
    new_scores = jnp.dot(k_all, q_new, preferred_element_type=jnp.float32) * scale
    live = jnp.arange(count, dtype=jnp.int32) < length
    new_scores = jnp.where(live, new_scores, masked_fill)
    self_score = jnp.dot(q_new, k_new, preferred_element_type=jnp.float32) * scale
    new_top = jnp.maximum(jnp.max(new_scores), self_score)
    new_weights = jnp.where(live, jnp.exp(new_scores - new_top), 0.0)
    own_weight = jnp.exp(self_score - new_top)
    new_total = jnp.sum(new_weights) + own_weight
    own_rounded = lax.optimization_barrier(own_weight.astype(jnp.bfloat16)).astype(jnp.float32)
    numer = jnp.dot(new_weights.astype(jnp.bfloat16), v_all, preferred_element_type=jnp.float32)
    numer = numer + own_rounded * v_new.astype(jnp.float32)
    return (prompt_out, (numer / new_total).astype(jnp.bfloat16))


def body(tokens, new_tokens, w_qkv, w_out, q_gain, k_gain, post_gain, lengths):
    seqs, pos_dev, width_local = tokens.shape
    heads_local = width_local // HD
    full_width = w_qkv.shape[1]
    n_seq = lax.axis_size("seq")
    pairs = seqs * heads_local
    assert pairs == n_seq
    prompt_rows = seqs * pos_dev
    full_len = pos_dev * n_seq
    flat_rows = tokens.reshape(prompt_rows, width_local)
    local_rows = jnp.concatenate([flat_rows, new_tokens], 0)
    all_rows = lax.all_gather(local_rows, "tp", axis=1, tiled=True)
    proj = jnp.einsum("tn,cnf->ctf", all_rows, w_qkv, preferred_element_type=jnp.float32)
    query_raw, key_raw = (proj[0], proj[1])
    query_sq, key_sq = lax.psum(
        (jnp.sum(query_raw * query_raw, -1), jnp.sum(key_raw * key_raw, -1)), "tp"
    )

    def normed(values, square_sum, gain):
        return values * lax.rsqrt(square_sum[:, None] / full_width + norm_eps) * gain

    seq_index = lax.axis_index("seq")
    query_pos = seq_index * pos_dev + jnp.arange(pos_dev, dtype=jnp.int32)
    row_pos = jnp.concatenate([jnp.tile(query_pos, seqs), lengths.astype(jnp.int32)], 0)
    rows_all = prompt_rows + seqs
    queries = rotate(
        normed(query_raw, query_sq, q_gain).reshape(rows_all, heads_local, HD), row_pos[:, None]
    ).astype(jnp.bfloat16)
    keys = rotate(
        normed(key_raw, key_sq, k_gain).reshape(rows_all, heads_local, HD), row_pos[:, None]
    ).astype(jnp.bfloat16)
    values = proj[2].astype(jnp.bfloat16).reshape(rows_all, heads_local, HD)
    qkv = jnp.stack([queries[:prompt_rows], keys[:prompt_rows], values[:prompt_rows]], 0)
    qkv = qkv.reshape(3, seqs, pos_dev, heads_local, HD).transpose(1, 3, 0, 2, 4)
    qkv = qkv.reshape(pairs, 3, pos_dev, HD)
    got = lax.all_to_all(qkv, "seq", 0, 0, tiled=True)
    full = got.transpose(1, 0, 2, 3).reshape(3, full_len, HD)
    owner = seq_index
    own_prompt = owner // heads_local
    new_q = queries[prompt_rows:].reshape(pairs, HD)[owner]
    new_k = keys[prompt_rows:].reshape(pairs, HD)[owner]
    new_v = values[prompt_rows:].reshape(pairs, HD)[owner]
    prompt_out, new_out = attend_pair(
        full[0], full[1], full[2], new_q, new_k, new_v, lengths[own_prompt]
    )
    pad = 8
    back = jnp.concatenate(
        [prompt_out.reshape(n_seq, pos_dev, HD), jnp.broadcast_to(new_out, (n_seq, pad, HD))], 1
    )
    ret = lax.all_to_all(back, "seq", 0, 0, tiled=True)
    ret = ret.reshape(seqs, heads_local, pos_dev + pad, HD)
    attn_rows = ret[:, :, :pos_dev].transpose(0, 2, 1, 3).reshape(prompt_rows, width_local)
    attn_new = ret[:, :, pos_dev].reshape(seqs, width_local)
    attention = jnp.concatenate([attn_rows, attn_new], 0)
    part = jnp.dot(attention, w_out, preferred_element_type=jnp.float32)
    summed = lax.psum_scatter(
        part.astype(jnp.bfloat16), "tp", scatter_dimension=1, tiled=True
    ).astype(jnp.float32)
    square = lax.psum(jnp.sum(summed * summed, -1), "tp")
    out = (
        local_rows.astype(jnp.float32)
        + summed * lax.rsqrt(square[:, None] / full_width + norm_eps) * post_gain
    ).astype(jnp.bfloat16)
    return (out[:prompt_rows].reshape(seqs, pos_dev, width_local), out[prompt_rows:])


def solution(mesh):
    in_specs = (
        P(None, "seq", "tp"),
        P(None, "tp"),
        P(None, None, "tp"),
        P("tp", None),
        P("tp"),
        P("tp"),
        P("tp"),
        P(),
    )
    out_specs = (P(None, "seq", "tp"), P(None, "tp"))
    return jax.shard_map(body, mesh=mesh, in_specs=in_specs, out_specs=out_specs, check_vma=False)
```

profile of v0, /device:TPU:4, one launch (start us, length us, event | category | flops | bytes accessed | tf_op | source)
XLA Modules:
  0.0 334.7 jit_solution(7153203666881482094)
XLA Ops:
  7.2 1.9 pad_maximum_fusion.2
  9.2 1.7 multiply_cosine_fusion
  11.0 92.7 %all-gather.2.cloned.1.call-done = bf16[516,4096]{1,0:T(8,128)(2,1)} async-done(((bf16[516,512]{1,0:T(8,128)(2,1)}), bf16[516,4096]{1,0:T(8,128)(2,1)}) %all-gather.2.cloned.1.call-update) | async-done | bytes 4227088 | tf_op jit(solution)/shard_map/all_gather | solution.py:62
  103.7 10.6 %fusion.45 = (bf16[3,516,512]{2,1,0:T(8,128)(2,1)S(1)}, f32[3,516,512]{2,1,0:T(8,128)S(1)}) fusion(bf16[3,4096,512]{2,1,0:T(8,128)(2,1)} %param.10, bf16[516,4096]{1,0:T(8,128)(2,1)} %all-gather.2.cloned.1.call-done), kind=kOutput, calls=%fused_computation.82 | convolution fusion | flops 6493575168 | bytes 21565440 | tf_op jit(solution)/shard_map/tn,cnf->ctf/dot_general | solution.py:63
  114.3 0.3 multiply_reduce_fusion.1
  114.7 0.8 copy-done.4
  115.5 0.1 stack.14
  115.7 0.9 copy.12
  116.6 0.4 squeeze.27
  116.9 0.4 squeeze.28
  117.3 18.3 %all-reduce = (f32[516]{0:T(1024)S(1)}, f32[516]{0:T(1024)S(1)}) all-reduce(f32[516]{0:T(1024)S(1)} %get-tuple-element.3, f32[516]{0:T(1024)S(1)} %get-tuple-element.2), channel_id=1, replica_groups=mesh['seq'=16,'tp'=8] {'tp'}, use_global_device_ids=true, to_apply=%region_3.0 | all-reduce | flops 1032 | bytes 8256 | tf_op jit(solution)/shard_map/psum | solution.py:65
  135.7 1.5 multiply_multiply_fusion.1
  137.2 1.5 multiply_multiply_fusion
  138.8 1.7 add_convert_fusion.1
  140.5 0.7 fusion.27
  141.3 0.1 copy.10
  141.4 0.7 fusion.26
  142.1 0.1 copy.11
  142.2 0.2 copy-done.2
  142.4 1.3 pad_maximum_fusion
  143.7 7.4 %all-to-all-start = ((bf16[16,3,128,128]{3,2,1,0:T(8,128)(2,1)}), bf16[16,3,128,128]{3,2,1,0:T(8,128)(2,1)S(1)}, u32[]{:S(2)}, u32[]{:S(2)}) async-start(bf16[16,3,128,128]{3,2,1,0:T(8,128)(2,1)} %bitcast.10), calls=%async_computation | async-start | bytes 3145728 | tf_op jit(solution)/shard_map/all_to_all | solution.py:86
  151.1 0.2 reduce-scatter.2.cloned.1.call-start
  151.4 0.6 dynamic_slice.12
  152.0 0.7 iota_compare_fusion.1
  152.6 0.7 slice.101
  153.3 0.8 pad_maximum_fusion.4
  154.1 0.1 pad_maximum_fusion.3
  154.2 0.6 fusion.34
  155.4 16.7 %all-to-all-done = bf16[16,3,128,128]{3,2,1,0:T(8,128)(2,1)S(1)} async-done(((bf16[16,3,128,128]{3,2,1,0:T(8,128)(2,1)}), bf16[16,3,128,128]{3,2,1,0:T(8,128)(2,1)S(1)}, u32[]{:S(2)}, u32[]{:S(2)}) %all-to-all-start) | async-done | bytes 1572896 | tf_op jit(solution)/shard_map/all_to_all | solution.py:86
  172.1 0.1 fusion.44
  172.2 0.2 fusion.38
  172.4 1.3 fusion.28
  174.4 1.3 fusion.29
  176.3 5.9 %fusion.1 = (f32[2048]{0:T(1024)S(1)}, f32[2048,2048]{0,1:T(8,128)S(1)}) fusion(pred[2048]{0:T(1024)(128)(4,1)S(1)} %iota_compare_fusion.1, bf16[2048,128]{1,0:T(8,128)(2,1)S(1)} %bitcast.92, bf16[2048,128]{1,0:T(8,128)(2,1)S(1)} %bitcast.88), kind=kOutput, calls=%fused_computation.4 | convolution fusion | flops 1094711296 | bytes 17836032 | tf_op jit(solution)/shard_map/dot_general | solution.py:26
  182.2 8.4 %fusion.6 = f32[2048]{0:T(1024)S(1)} fusion(f32[2048]{0:T(1024)S(1)} %get-tuple-element.23, f32[2048,2048]{0,1:T(8,128)S(1)} %get-tuple-element.24, pred[2048]{0:T(1024)(128)(4,1)S(1)} %iota_compare_fusion.1), kind=kLoop, calls=%fused_computation.10 | loop fusion | flops 29358080 | bytes 16795648 | tf_op jit(solution)/shard_map/reduce_sum | solution.py:33
  190.6 3.5 %fusion.10 = bf16[2048,128]{1,0:T(8,128)(2,1)S(1)} fusion(bf16[2048,128]{1,0:T(8,128)(2,1)S(1)} %bitcast.85, f32[2048]{0:T(1024)S(1)} %get-tuple-element.23, f32[2048,2048]{0,1:T(8,128)S(1)} %get-tuple-element.24, pred[2048]{0:T(1024)(128)(4,1)S(1)} %iota_compare_fusion.1, f32[2048]{0:T(1024)S(1)} %fusion.6), kind=kOutput, calls=%fused_computation.12 | convolution fusion | flops 1103626240 | bytes 17844224 | tf_op jit(solution)/shard_map/dot_general | solution.py:35
  194.1 0.2 fusion.18
  194.4 17.3 %all_to_all.10 = bf16[16,136,128]{2,1,0:T(8,128)(2,1)S(1)} all-to-all(bf16[16,136,128]{2,1,0:T(8,128)(2,1)S(1)} %pad_maximum_fusion.1), channel_id=1, replica_groups=mesh['seq'=16,'tp'=8] {'seq'}, dimensions={0} | all-to-all | bytes 1114112 | tf_op jit(solution)/shard_map/all_to_all | solution.py:100
  211.8 0.2 slice_bitcast_fusion
  212.0 0.2 copy.14
  212.2 0.1 copy.22
  212.3 4.4 %convolution_convert_fusion = bf16[516,4096]{1,0:T(8,128)(2,1)} fusion(bf16[512,4096]{1,0:T(8,128)(2,1)S(1)} %copy-done.10, bf16[4,512]{1,0:T(4,128)(2,1)S(1)} %bitcast.98, bf16[512,512]{1,0:T(8,128)(2,1)S(1)} %bitcast.91), kind=kOutput, calls=%fused_computation.7 | convolution fusion | flops 2167431168 | bytes 8949760 | tf_op jit(solution)/shard_map/dot_general | solution.py:105
  216.7 89.1 %reduce-scatter.2.cloned.1.call-done = bf16[516,512]{1,0:T(8,128)(2,1)} async-done(((bf16[516,4096]{1,0:T(8,128)(2,1)}), bf16[516,512]{1,0:T(8,128)(2,1)}) %reduce-scatter.2.cloned.1.call-update) | async-done | bytes 528400 | tf_op jit(solution)/shard_map/reduce_scatter | solution.py:106
  305.8 1.2 fusion.19
  307.0 18.0 %psum.23 = f32[516]{0:T(1024)S(1)} all-reduce(f32[516]{0:T(1024)S(1)} %fusion.19), channel_id=1, replica_groups=mesh['seq'=16,'tp'=8] {'tp'}, use_global_device_ids=true, to_apply=%region_10.11 | all-reduce | flops 516 | bytes 4128 | tf_op jit(solution)/shard_map/psum | solution.py:109
  325.1 1.3 fusion.22
  326.4 0.6 slice.105
  327.0 0.8 slice.104
  (37 shorter events, 0.4 us)
Async XLA Ops:
  7.2 2.0 copy-start.9
  7.2 96.5 %all-gather.2.cloned.1.call-start = ((), (), s32[]{:S(2)}) async-start(), calls=%async_computation.3 | async-start | bytes 4792320 | tf_op jit(solution)/shard_map/all_gather | solution.py:62
  114.3 1.2 copy-start.4
  116.9 18.8 %copy-start.6 = (f32[512]{0:T(512)S(1)}, f32[512]{0:T(512)}, u32[]{:S(2)}) copy-start(f32[512]{0:T(512)} %param.12) | copy-start | bytes 6148
  117.3 19.9 %copy-start.7 = (f32[512]{0:T(512)S(1)}, f32[512]{0:T(512)}, u32[]{:S(2)}) copy-start(f32[512]{0:T(512)} %param.13) | copy-start | bytes 6148
  137.2 1.6 copy-start.3
  140.5 1.6 copy-start
  141.4 1.0 copy-start.2
  143.7 28.4 %all-to-all-start = ((bf16[16,3,128,128]{3,2,1,0:T(8,128)(2,1)}), bf16[16,3,128,128]{3,2,1,0:T(8,128)(2,1)S(1)}, u32[]{:S(2)}, u32[]{:S(2)}) async-start(bf16[16,3,128,128]{3,2,1,0:T(8,128)(2,1)} %bitcast.10), calls=%async_computation | async-start | bytes 3145728 | tf_op jit(solution)/shard_map/all_to_all | solution.py:86
  151.1 154.7 %reduce-scatter.2.cloned.1.call-start = ((), (), s32[]{:S(2)}) async-start(), calls=%async_computation.4 | async-start | bytes 4792320 | tf_op jit(solution)/shard_map/reduce_scatter | solution.py:106
  194.4 17.9 %copy-start.10 = (bf16[512,4096]{1,0:T(8,128)(2,1)S(1)}, bf16[512,4096]{1,0:T(8,128)(2,1)}, u32[]{:S(2)}) copy-start(bf16[512,4096]{1,0:T(8,128)(2,1)} %param.11) | copy-start | bytes 12582916
  216.6 108.4 %copy-start.1 = (bf16[4,128,512]{2,1,0:T(8,128)(2,1)S(1)}, bf16[4,128,512]{2,1,0:T(8,128)(2,1)}, u32[]{:S(2)}) copy-start(bf16[4,128,512]{2,1,0:T(8,128)(2,1)} %param.8) | copy-start | bytes 1572868
  216.6 108.4 %copy-start.5 = (bf16[4,512]{1,0:T(4,128)(2,1)S(1)}, bf16[4,512]{1,0:T(4,128)(2,1)}, u32[]{:S(2)}) copy-start(bf16[4,512]{1,0:T(4,128)(2,1)} %param.9) | copy-start | bytes 12292
  216.6 108.4 %copy-start.8 = (f32[512]{0:T(512)S(1)}, f32[512]{0:T(512)}, u32[]{:S(2)}) copy-start(f32[512]{0:T(512)} %param.14) | copy-start | bytes 6148
Sparse Core Ops, SparseCore 0:
  9.7 93.9 all-gather.1
  216.8 88.9 reduce-scatter.1
where the time goes:
time: 335 us
  waiting for transfers between devices  199 us (59%)
  blocking collectives  53.6 us (16%)
  other arithmetic  27.2 us (8%)
  matrix products  24.8 us (7%)
  between operations  16.4 us (5%)
  starting transfers between devices  7.66 us (2%)
  local copies, waits for them, and re-layouts  6.41 us (2%)
    all_gather x1, waiting for transfers between devices, body(): all_rows = lax.all_gather(local_rows, 'tp', axis=1, tiled=True)  92.7 us
    reduce_scatter x1, waiting for transfers between devices, body(): lax.psum_scatter(part.astype(jnp.bfloat16), 'tp', scatter_dimension=1, ti...  89.1 us
    psum x1, blocking collectives, body(): lax.psum((jnp.sum(query_raw * query_raw, -1), jnp.sum(key_raw * key_raw,...  18.3 us
    psum x1, blocking collectives, body(): square = lax.psum(jnp.sum(summed * summed, -1), 'tp')  18 us
    all_to_all x1, blocking collectives, body(): ret = lax.all_to_all(back, 'seq', 0, 0, tiled=True)  17.3 us
    all_to_all x1, waiting for transfers between devices, body(): got = lax.all_to_all(qkv, 'seq', 0, 0, tiled=True)  16.7 us
    dot_general x1, matrix products, body(): jnp.einsum('tn,cnf->ctf', all_rows, w_qkv, preferred_element_type=jnp.flo...  10.6 us
    reduce_sum x1, other arithmetic, attend_pair(): total = jnp.sum(weights, -1, keepdims=True)  8.42 us
  transfers between devices with their start and end apart: 3, of which 3 were waited for; matrix products, arithmetic and copies ran while one was open for 2% of the time, Pallas kernels for 0%

commit v1 on v0

--- a/solution.py
+++ b/solution.py
@@ -106,7 +106,7 @@
     summed = lax.psum_scatter(
         part.astype(jnp.bfloat16), "tp", scatter_dimension=1, tiled=True
     ).astype(jnp.float32)
-    square = lax.psum(jnp.sum(summed * summed, -1), "tp")
+    square = jnp.sum(lax.all_gather(jnp.sum(summed * summed, -1), "tp"), axis=0)
     out = (
         local_rows.astype(jnp.float32)
         + summed * lax.rsqrt(square[:, None] / full_width + norm_eps) * post_gain

time: 335 us -> 353 us (1.054)
  blocking collectives: 53.6 us -> 68.2 us
    unnamed x0 -> x1, blocking collectives: none -> 32.6 us
    psum x1 -> x0, blocking collectives: 18 us -> none  [body(): square = lax.psum(jnp.sum(summed * summed, -1), 'tp')]
where the time goes in v1:
time: 353 us; the launch traced here: 352 us
  waiting for transfers between devices  197 us (56%)
  blocking collectives  68.2 us (19%)
  other arithmetic  28.7 us (8%)
  matrix products  26.4 us (7%)
  between operations  17.1 us (5%)
  starting transfers between devices  7.67 us (2%)
  local copies, waits for them, and re-layouts  7.46 us (2%)
    all_gather x1, waiting for transfers between devices, body(): all_rows = lax.all_gather(local_rows, 'tp', axis=1, tiled=True)  92.7 us
    reduce_scatter x1, waiting for transfers between devices, body(): lax.psum_scatter(part.astype(jnp.bfloat16), 'tp', scatter_dimension=1, ti...  87.3 us
    unnamed x1, blocking collectives  32.6 us
    psum x1, blocking collectives, body(): lax.psum((jnp.sum(query_raw * query_raw, -1), jnp.sum(key_raw * key_raw,...  18.3 us
    all_to_all x1, blocking collectives, body(): ret = lax.all_to_all(back, 'seq', 0, 0, tiled=True)  17.3 us
    all_to_all x1, waiting for transfers between devices, body(): got = lax.all_to_all(qkv, 'seq', 0, 0, tiled=True)  16.7 us
    dot_general x1, matrix products, body(): jnp.einsum('tn,cnf->ctf', all_rows, w_qkv, preferred_element_type=jnp.flo...  12.3 us
    reduce_sum x1, other arithmetic, attend_pair(): total = jnp.sum(weights, -1, keepdims=True)  8.42 us
  transfers between devices with their start and end apart: 3, of which 3 were waited for; matrix products, arithmetic and copies ran while one was open for 2% of the time, Pallas kernels for 0%

profile of v1, /device:TPU:4, one launch (start us, length us, event | category | flops | bytes accessed | tf_op | source)
XLA Modules:
  0.0 352.4 jit_solution(13190300521382007325)
XLA Ops:
  7.2 1.9 pad_maximum_fusion.2
  9.2 1.7 multiply_cosine_fusion
  10.9 92.7 %all-gather.3.cloned.1.call-done = bf16[516,4096]{1,0:T(8,128)(2,1)} async-done(((bf16[516,512]{1,0:T(8,128)(2,1)}), bf16[516,4096]{1,0:T(8,128)(2,1)}) %all-gather.3.cloned.1.call-update) | async-done | bytes 4227088 | tf_op jit(solution)/shard_map/all_gather | solution.py:62
  103.7 12.3 %fusion.45 = (bf16[3,516,512]{2,1,0:T(8,128)(2,1)S(1)}, f32[3,516,512]{2,1,0:T(8,128)}) fusion(bf16[3,4096,512]{2,1,0:T(8,128)(2,1)} %param.10, bf16[516,4096]{1,0:T(8,128)(2,1)} %all-gather.3.cloned.1.call-done), kind=kOutput, calls=%fused_computation.82 | convolution fusion | flops 6493575168 | bytes 21565440 | tf_op jit(solution)/shard_map/tn,cnf->ctf/dot_general | solution.py:63
  116.0 0.1 stack.14
  116.2 1.1 copy.17
  117.3 1.9 multiply_reduce_fusion.1
  119.2 0.4 squeeze.27
  119.6 0.4 squeeze.28
  120.0 18.3 %all-reduce.1 = (f32[516]{0:T(1024)S(1)}, f32[516]{0:T(1024)S(1)}) all-reduce(f32[516]{0:T(1024)S(1)} %get-tuple-element.3, f32[516]{0:T(1024)S(1)} %get-tuple-element.2), channel_id=1, replica_groups=mesh['seq'=16,'tp'=8] {'tp'}, use_global_device_ids=true, to_apply=%region_3.0 | all-reduce | flops 1032 | bytes 8256 | tf_op jit(solution)/shard_map/psum | solution.py:65
  138.4 1.5 multiply_multiply_fusion.1
  139.9 1.5 multiply_multiply_fusion
  141.5 1.7 add_convert_fusion.1
  143.2 0.7 fusion.26
  143.9 0.1 copy.16
  144.1 0.7 fusion.27
  144.8 0.1 copy.15
  144.9 0.2 copy-done.2
  145.1 1.3 pad_maximum_fusion
  146.4 7.4 %all-to-all-start = ((bf16[16,3,128,128]{3,2,1,0:T(8,128)(2,1)}), bf16[16,3,128,128]{3,2,1,0:T(8,128)(2,1)S(1)}, u32[]{:S(2)}, u32[]{:S(2)}) async-start(bf16[16,3,128,128]{3,2,1,0:T(8,128)(2,1)} %bitcast.10), calls=%async_computation | async-start | bytes 3145728 | tf_op jit(solution)/shard_map/all_to_all | solution.py:86
  153.8 0.2 reduce-scatter.2.cloned.1.call-start
  154.1 0.6 dynamic_slice.12
  154.6 0.7 iota_compare_fusion.1
  155.3 0.7 slice.101
  156.0 0.8 pad_maximum_fusion.4
  156.9 0.6 fusion.34
  158.1 16.7 %all-to-all-done = bf16[16,3,128,128]{3,2,1,0:T(8,128)(2,1)S(1)} async-done(((bf16[16,3,128,128]{3,2,1,0:T(8,128)(2,1)}), bf16[16,3,128,128]{3,2,1,0:T(8,128)(2,1)S(1)}, u32[]{:S(2)}, u32[]{:S(2)}) %all-to-all-start) | async-done | bytes 1572896 | tf_op jit(solution)/shard_map/all_to_all | solution.py:86
  174.8 0.1 fusion.44
  174.9 0.2 fusion.38
  175.1 1.3 fusion.28
  177.0 1.3 fusion.29
  179.0 5.9 %fusion.1 = (f32[2048]{0:T(1024)S(1)}, f32[2048,2048]{0,1:T(8,128)S(1)}) fusion(pred[2048]{0:T(1024)(128)(4,1)S(1)} %iota_compare_fusion.1, bf16[2048,128]{1,0:T(8,128)(2,1)S(1)} %bitcast.93, bf16[2048,128]{1,0:T(8,128)(2,1)S(1)} %bitcast.89), kind=kOutput, calls=%fused_computation.4 | convolution fusion | flops 1094711296 | bytes 17836032 | tf_op jit(solution)/shard_map/dot_general | solution.py:26
  184.9 8.4 %fusion.6 = f32[2048]{0:T(1024)S(1)} fusion(f32[2048]{0:T(1024)S(1)} %get-tuple-element.23, f32[2048,2048]{0,1:T(8,128)S(1)} %get-tuple-element.24, pred[2048]{0:T(1024)(128)(4,1)S(1)} %iota_compare_fusion.1), kind=kLoop, calls=%fused_computation.10 | loop fusion | flops 29358080 | bytes 16795648 | tf_op jit(solution)/shard_map/reduce_sum | solution.py:33
  193.3 3.5 fusion.10
  196.8 0.2 fusion.18
  197.1 17.3 %all_to_all.10 = bf16[16,136,128]{2,1,0:T(8,128)(2,1)S(1)} all-to-all(bf16[16,136,128]{2,1,0:T(8,128)(2,1)S(1)} %pad_maximum_fusion.1), channel_id=1, replica_groups=mesh['seq'=16,'tp'=8] {'seq'}, dimensions={0} | all-to-all | bytes 1114112 | tf_op jit(solution)/shard_map/all_to_all | solution.py:100
  214.5 0.2 slice_bitcast_fusion
  214.7 0.2 copy.19
  214.9 4.4 %convolution_convert_fusion = bf16[516,4096]{1,0:T(8,128)(2,1)} fusion(bf16[512,4096]{1,0:T(8,128)(2,1)S(1)} %copy-done.10, bf16[4,512]{1,0:T(4,128)(2,1)S(1)} %bitcast.99, bf16[512,512]{1,0:T(8,128)(2,1)S(1)} %bitcast.92), kind=kOutput, calls=%fused_computation.7 | convolution fusion | flops 2167431168 | bytes 8949760 | tf_op jit(solution)/shard_map/dot_general | solution.py:105
  219.3 0.6 copy-done.11
  220.0 0.6 dynamic-slice
  221.2 87.3 %reduce-scatter.2.cloned.1.call-done = bf16[516,512]{1,0:T(8,128)(2,1)} async-done(((bf16[516,4096]{1,0:T(8,128)(2,1)}), bf16[516,512]{1,0:T(8,128)(2,1)}) %reduce-scatter.2.cloned.1.call-update) | async-done | bytes 528400 | tf_op jit(solution)/shard_map/reduce_scatter | solution.py:106
  308.5 1.2 fusion.19
  309.7 0.3 dynamic-update-slice
  310.0 32.6 %all-reduce = f32[4128]{0:T(1024)S(1)} all-reduce(f32[4128]{0:T(1024)S(1)} %dynamic-update-slice), channel_id=2, replica_groups=mesh['seq'=16,'tp'=8] {'tp'}, use_global_device_ids=true, to_apply=%add | all-reduce | flops 4128 | bytes 33024
  342.8 1.3 fusion.22
  344.1 0.8 slice.104
  344.9 0.6 slice.105
  (44 shorter events, 0.7 us)
Async XLA Ops:
  7.2 2.0 copy-start.9
  7.2 96.5 %all-gather.3.cloned.1.call-start = ((), (), s32[]{:S(2)}) async-start(), calls=%async_computation.3 | async-start | bytes 4792320 | tf_op jit(solution)/shard_map/all_gather | solution.py:62
  116.0 1.4 copy-start.4
  119.6 18.7 %copy-start.6 = (f32[512]{0:T(512)S(1)}, f32[512]{0:T(512)}, u32[]{:S(2)}) copy-start(f32[512]{0:T(512)} %param.12) | copy-start | bytes 6148
  120.0 19.9 %copy-start.7 = (f32[512]{0:T(512)S(1)}, f32[512]{0:T(512)}, u32[]{:S(2)}) copy-start(f32[512]{0:T(512)} %param.13) | copy-start | bytes 6148
  139.9 1.6 copy-start.3
  143.2 1.6 copy-start
  144.0 1.0 copy-start.2
  146.4 28.4 %all-to-all-start = ((bf16[16,3,128,128]{3,2,1,0:T(8,128)(2,1)}), bf16[16,3,128,128]{3,2,1,0:T(8,128)(2,1)S(1)}, u32[]{:S(2)}, u32[]{:S(2)}) async-start(bf16[16,3,128,128]{3,2,1,0:T(8,128)(2,1)} %bitcast.10), calls=%async_computation | async-start | bytes 3145728 | tf_op jit(solution)/shard_map/all_to_all | solution.py:86
  153.8 154.7 %reduce-scatter.2.cloned.1.call-start = ((), (), s32[]{:S(2)}) async-start(), calls=%async_computation.4 | async-start | bytes 4792320 | tf_op jit(solution)/shard_map/reduce_scatter | solution.py:106
  197.1 17.9 %copy-start.10 = (bf16[512,4096]{1,0:T(8,128)(2,1)S(1)}, bf16[512,4096]{1,0:T(8,128)(2,1)}, u32[]{:S(2)}) copy-start(bf16[512,4096]{1,0:T(8,128)(2,1)} %param.11) | copy-start | bytes 12582916
  219.3 0.7 copy-start.11
  219.3 123.5 %copy-start.1 = (bf16[4,128,512]{2,1,0:T(8,128)(2,1)S(1)}, bf16[4,128,512]{2,1,0:T(8,128)(2,1)}, u32[]{:S(2)}) copy-start(bf16[4,128,512]{2,1,0:T(8,128)(2,1)} %param.8) | copy-start | bytes 1572868
  219.3 123.5 %copy-start.5 = (bf16[4,512]{1,0:T(4,128)(2,1)S(1)}, bf16[4,512]{1,0:T(4,128)(2,1)}, u32[]{:S(2)}) copy-start(bf16[4,512]{1,0:T(4,128)(2,1)} %param.9) | copy-start | bytes 12292
  219.3 123.5 %copy-start.8 = (f32[512]{0:T(512)S(1)}, f32[512]{0:T(512)}, u32[]{:S(2)}) copy-start(f32[512]{0:T(512)} %param.14) | copy-start | bytes 6148
Sparse Core Ops, SparseCore 0:
  9.7 93.9 all-gather.2
  219.5 88.9 reduce-scatter.1
